TPU v7x, 128 devices: a whole 4x4x4 slice. The times are simulated.
128 devices in a mesh: tok: 8 (over z, core), wid: 16 (over y, x).
Axes of the slice: x: 4, y: 4, z: 4, core: 2. Of those that a mesh axis runs over, the one named last changes fastest.
Arguments:
- tokens: bfloat16 [8192, 3072], P('tok', 'wid'), may hold values from -6 to 6
- defect_mask: int32 [8192], P('tok'), may hold values 0 or 1
- timestep: int32 [1], replicated, may hold values from 0 to 999
- mask_embed: bfloat16 [3072], P('wid'), may hold values from -6 to 6
- mod_weight: bfloat16 [256, 3, 3072], P(None, None, 'wid'), may hold values from -0.375 to 0.375
- w_qkv: bfloat16 [3072, 3, 2048], P('tok', None, 'wid'), may hold values from -1.4614179 to 1.4614179, as said below
- w_out: bfloat16 [2048, 3072], P('wid'), may hold values from -0.125 to 0.125
Outputs:
- block_out: bfloat16 [8192, 3072], P('tok', 'wid')
Inputs may be any that keep to these rules, and one draw needn't show every extreme that they name: `w_qkv`: entries are at most 81 / sqrt(3072) in magnitude.
All inputs are finite; a program needn't handle non-finite values. No bound on the sum of `defect_mask` on one device may be relied on, other than what follows from the above.
Results may differ from a plain program's by a relative error of at most 0.011.
Values may be sent and summed in bfloat16 or wider, within the bound.
No kernel may reach another device: no remote copies, remote signals or barrier semaphores. Data moves between devices by JAX's collectives and lax.ppermute only.
A program may use at most 128 MiB of HBM per device.

v0:
```python
import math
import jax
import jax.numpy as jnp
from jax import lax
from jax.sharding import PartitionSpec as P

D = 3072
DH = 128
TEMB = 256


def finish_rows(values, row_mean, row_var, shift_row, scale_row):
    normal = (values - row_mean) * lax.rsqrt(row_var + 1e-06)
    return (normal * (1.0 + scale_row.astype(jnp.float32)) + shift_row.astype(jnp.float32)).astype(
        jnp.bfloat16
    )


def body(tokens, defect_mask, timestep, mask_embed, mod_weight, w_qkv, w_out):
    tok_rows = tokens.shape[0]
    residual_in = (
        tokens.astype(jnp.float32)
        + defect_mask.astype(jnp.float32)[:, None] * mask_embed.astype(jnp.float32)[None, :]
    ).astype(jnp.bfloat16)
    w_cols = lax.all_to_all(w_out, "wid", split_axis=1, concat_axis=0, tiled=True)
    tok_count = lax.axis_size("tok")
    w_copies = jnp.broadcast_to(w_qkv[None], (tok_count,) + w_qkv.shape)
    w_full = lax.all_to_all(w_copies, "tok", split_axis=0, concat_axis=0, tiled=True)
    w_full = w_full.reshape((tok_count * w_qkv.shape[0],) + w_qkv.shape[1:])
    half_width = TEMB // 2
    frequency = jnp.exp(-math.log(10000.0) * jnp.arange(half_width, dtype=jnp.float32) / half_width)
    angles = timestep.astype(jnp.float32)[0] * frequency
    embedding = jnp.concatenate([jnp.cos(angles), jnp.sin(angles)])
    modulation = jnp.einsum(
        "e,ecf->cf",
        jax.nn.silu(embedding),
        mod_weight.astype(jnp.float32),
        precision=lax.Precision.HIGHEST,
    ).astype(jnp.bfloat16)
    extra = jnp.zeros((16, residual_in.shape[1]), jnp.bfloat16).at[:2].set(modulation[:2])
    packed = lax.all_gather(
        jnp.concatenate([residual_in, extra], axis=0), "wid", axis=1, tiled=True
    )
    residual_full = packed[:tok_rows]
    shift_scale = packed[tok_rows : tok_rows + 2]
    values = residual_full.astype(jnp.float32)
    row_mean = jnp.mean(values, axis=1, keepdims=True)
    row_var = jnp.mean(values * values, axis=1, keepdims=True) - row_mean * row_mean
    normed = finish_rows(
        values, row_mean, row_var, shift_scale[0][None, :], shift_scale[1][None, :]
    )
    qkv = jnp.einsum("td,dcf->tcf", normed, w_full, preferred_element_type=jnp.float32).astype(
        jnp.bfloat16
    )
    qkv, w_cols = lax.optimization_barrier((qkv, w_cols))
    queries = qkv[:, 0]
    key_values = lax.all_gather(qkv[:, 1:3], "tok", axis=0, tiled=True)
    key_part = key_values[:, 0]
    value_part = key_values[:, 1]
    score_scale = DH ** (-0.5)
    scores = jnp.dot(queries, key_part.T, preferred_element_type=jnp.float32) * score_scale
    shifted = jnp.exp(scores - jnp.max(scores, axis=1, keepdims=True))
    row_sum = jnp.sum(shifted, axis=1, keepdims=True)
    numer = jnp.dot(shifted.astype(jnp.bfloat16), value_part, preferred_element_type=jnp.float32)
    attended = (numer / row_sum).astype(jnp.bfloat16)
    attended_full = lax.all_gather(attended, "wid", axis=1, tiled=True)
    projected = jnp.dot(attended_full, w_cols, preferred_element_type=jnp.float32)
    return (
        residual_in.astype(jnp.float32) + modulation[2].astype(jnp.float32)[None, :] * projected
    ).astype(jnp.bfloat16)


def solution(mesh):
    return jax.shard_map(
        body,
        mesh=mesh,
        in_specs=(
            P("tok", "wid"),
            P("tok"),
            P(),
            P("wid"),
            P(None, None, "wid"),
            P("tok", None, "wid"),
            P("wid", None),
        ),
        out_specs=P("tok", "wid"),
        check_vma=False,
    )
```

profile of v0, /device:TPU:0, one launch (start us, length us, event | category | flops | bytes accessed | tf_op | source)
XLA Modules:
  0.0 239.3 jit_solution(12590052405980159787)
XLA Ops:
  6.5 0.0 copy-start
  6.5 0.0 all-gather.4.cloned.1.call-start
  7.3 0.7 convert_element_type.48
  8.0 0.7 convert_element_type.47
  8.7 0.0 copy-done
  8.7 0.3 fusion.32
  9.0 0.2 copy.16
  9.2 1.2 add_convert_fusion
  10.4 0.0 copy-start.2
  10.4 0.7 copy-done.2
  11.1 0.8 fusion.26
  11.9 0.0 all-gather.4.cloned.1.call-update
  11.9 1.5 copy.14
  13.4 25.8 %all_to_all.24 = bf16[128,16,192]{0,2,1:T(8,128)(2,1)S(1)} all-to-all(bf16[128,16,192]{0,2,1:T(8,128)(2,1)S(1)} %bitcast.41), channel_id=1, replica_groups=mesh['tok'=8,'wid'=16] {'wid'}, dimensions={1} | all-to-all | bytes 1572864 | tf_op jit(solution)/shard_map/all_to_all | solution.py:25
  39.3 2.9 %broadcast_in_dim.2 = bf16[8,384,3,128]{3,1,2,0:T(8,128)(2,1)} broadcast(bf16[384,3,128]{2,0,1:T(8,128)(2,1)} %param.14), dimensions={1,2,3} | broadcast | bytes 2654208 | tf_op jit(solution)/shard_map/broadcast_in_dim | solution.py:27
  42.2 5.8 %all-to-all-start = ((bf16[8,384,3,128]{3,1,2,0:T(8,128)(2,1)}), bf16[8,384,3,128]{3,1,2,0:T(8,128)(2,1)S(1)}, u32[]{:S(2)}, u32[]{:S(2)}) async-start(bf16[8,384,3,128]{3,1,2,0:T(8,128)(2,1)} %broadcast_in_dim.2), calls=%async_computation | async-start | bytes 4718592 | tf_op jit(solution)/shard_map/all_to_all | solution.py:28
  48.0 0.0 all-gather.6.cloned.1.call-start
  48.1 1.0 copy_bitcast_fusion
  49.1 28.9 %all-to-all-done = bf16[8,384,3,128]{3,1,2,0:T(8,128)(2,1)S(1)} async-done(((bf16[8,384,3,128]{3,1,2,0:T(8,128)(2,1)}), bf16[8,384,3,128]{3,1,2,0:T(8,128)(2,1)S(1)}, u32[]{:S(2)}, u32[]{:S(2)}) %all-to-all-start) | async-done | bytes 2359328 | tf_op jit(solution)/shard_map/all_to_all | solution.py:28
  78.0 1.6 copy.12
  79.6 3.2 %all-gather.4.cloned.1.call-done = bf16[1040,3072]{0,1:T(8,128)(2,1)} async-done(((bf16[1040,192]{0,1:T(8,128)(2,1)}), bf16[1040,3072]{0,1:T(8,128)(2,1)}) %all-gather.4.cloned.1.call-update) | async-done | bytes 6389776 | tf_op jit(solution)/shard_map/all_gather | solution.py:41
  82.9 0.0 copy-start.1
  82.9 4.6 %convert_reduce_fusion = (f32[1024]{0:T(1024)S(1)}, f32[1024]{0:T(1024)S(1)}) fusion(bf16[1040,3072]{0,1:T(8,128)(2,1)} %all-gather.4.cloned.1.call-done), kind=kLoop, calls=%fused_computation.6 | loop fusion | flops 12580864 | bytes 6299648 | tf_op jit(solution)/shard_map/reduce_sum | solution.py:47
  87.5 2.5 %add_reduce_fusion = (f32[3072]{0:T(1024)S(1)}, f32[3072]{0:T(1024)S(1)}) fusion(bf16[1040,3072]{0,1:T(8,128)(2,1)} %all-gather.4.cloned.1.call-done), kind=kLoop, calls=%fused_computation.20 | loop fusion | flops 9216 | bytes 36864 | tf_op jit(solution)/shard_map/add | solution.py:14
  90.0 0.0 copy-done.1
  90.0 5.6 %fusion.14 = bf16[1024,3,128]{2,0,1:T(8,128)(2,1)S(1)} fusion(bf16[3072,3,128]{2,0,1:T(8,128)(2,1)} %bitcast.42, f32[3072]{0:T(1024)S(1)} %get-tuple-element.24, f32[3072]{0:T(1024)S(1)} %get-tuple-element.23, f32[1024]{0:T(1024)S(1)} %get-tuple-element.26, f32[1024]{0:T(1024)S(1)} %get-tuple-element.25, bf16[1040,3072]{0,1:T(8,128)(2,1)S(1)} %copy-done.1), kind=kOutput, calls=%fused_computation.21 | convolution fusion | flops 2435186688 | bytes 9469952 | tf_op jit(solution)/shard_map/td,dcf->tcf/dot_general | solution.py:52
  95.6 0.8 slice.52
  96.4 0.0 all-gather.6.cloned.1.call-update
  96.4 0.2 all-gather.8.cloned.1.call-start
  96.7 31.9 %all-gather.6.cloned.1.call-done = bf16[8192,2,128]{2,0,1:T(8,128)(2,1)} async-done(((bf16[1024,2,128]{2,0,1:T(8,128)(2,1)}), bf16[8192,2,128]{2,0,1:T(8,128)(2,1)}) %all-gather.6.cloned.1.call-update) | async-done | bytes 4194320 | tf_op jit(solution)/shard_map/all_gather | solution.py:57
  128.6 14.6 %multiply_reduce_fusion = (f32[1024]{0:T(1024)S(1)}, f32[1024,8192]{1,0:T(8,128)}) fusion(bf16[8192,2,128]{2,0,1:T(8,128)(2,1)} %all-gather.6.cloned.1.call-done, bf16[1024,3,128]{2,0,1:T(8,128)(2,1)S(1)} %fusion.14), kind=kOutput, calls=%fused_computation.1 | convolution fusion | flops 2164259840 | bytes 35917824 | tf_op jit(solution)/shard_map/dot_general | solution.py:61
  143.2 0.0 copy-start.4
  143.2 14.3 %fusion = f32[1024]{0:T(1024)S(1)} fusion(f32[1024,8192]{1,0:T(8,128)} %get-tuple-element.28, f32[1024]{0:T(1024)S(1)} %get-tuple-element.27), kind=kLoop, calls=%fused_computation.2 | loop fusion | flops 25164800 | bytes 33562624 | tf_op jit(solution)/shard_map/reduce_sum | solution.py:63
  157.5 0.0 copy-done.4
  157.5 0.0 copy-start.3
  157.5 0.0 copy-start.5
  157.5 14.2 %fusion.22 = bf16[1024,128]{1,0:T(8,128)(2,1)} fusion(bf16[8192,2,128]{2,0,1:T(8,128)(2,1)S(1)} %copy-done.4, f32[1024,8192]{1,0:T(8,128)} %get-tuple-element.28, f32[1024]{0:T(1024)S(1)} %get-tuple-element.27, f32[1024]{0:T(1024)S(1)} %fusion), kind=kOutput, calls=%fused_computation.26 | convolution fusion | flops 2172911616 | bytes 35921920 | tf_op jit(solution)/shard_map/dot_general | solution.py:64
  171.7 0.0 all-gather.8.cloned.1.call-update
  171.7 0.2 convert_reduce_fusion.2
  171.9 56.4 %all-gather.8.cloned.1.call-done = bf16[1024,2048]{1,0:T(8,128)(2,1)} async-done(((bf16[1024,128]{1,0:T(8,128)(2,1)}), bf16[1024,2048]{1,0:T(8,128)(2,1)}) %all-gather.8.cloned.1.call-update) | async-done | bytes 4194320 | tf_op jit(solution)/shard_map/all_gather | solution.py:66
  228.3 0.0 copy-done.3
  228.3 0.0 copy-done.5
  228.3 4.5 %fusion.18 = bf16[1024,192]{0,1:T(8,128)(2,1)} fusion(bf16[1024,2048]{1,0:T(8,128)(2,1)} %all-gather.8.cloned.1.call-done, bf16[2048,192]{0,1:T(8,128)(2,1)S(1)} %copy-done.5, bf16[1024,192]{0,1:T(8,128)(2,1)S(1)} %copy-done.3, f32[192]{0:T(256)S(1)} %convert_reduce_fusion.2), kind=kOutput, calls=%fused_computation.24 | convolution fusion | flops 806092800 | bytes 5767936 | tf_op jit(solution)/shard_map/dot_general | solution.py:67
  (3 shorter events, 0.1 us)
Async XLA Ops:
  6.5 2.1 copy-start
  6.5 76.3 %all-gather.4.cloned.1.call-start = ((), (), s32[]{:S(2)}) async-start(), calls=%async_computation.2 | async-start | bytes 7520256 | tf_op jit(solution)/shard_map/all_gather | solution.py:41
  10.4 0.7 copy-start.2
  42.2 35.8 %all-to-all-start = ((bf16[8,384,3,128]{3,1,2,0:T(8,128)(2,1)}), bf16[8,384,3,128]{3,1,2,0:T(8,128)(2,1)S(1)}, u32[]{:S(2)}, u32[]{:S(2)}) async-start(bf16[8,384,3,128]{3,1,2,0:T(8,128)(2,1)} %broadcast_in_dim.2), calls=%async_computation | async-start | bytes 4718592 | tf_op jit(solution)/shard_map/all_to_all | solution.py:28
  48.0 80.5 %all-gather.6.cloned.1.call-start = ((), (), s32[]{:S(2)}) async-start(), calls=%async_computation.3 | async-start | bytes 4718592 | tf_op jit(solution)/shard_map/all_gather | solution.py:57
  82.9 7.1 %copy-start.1 = (bf16[1040,3072]{0,1:T(8,128)(2,1)S(1)}, bf16[1040,3072]{0,1:T(8,128)(2,1)}, u32[]{:S(2)}) copy-start(bf16[1040,3072]{0,1:T(8,128)(2,1)} %all-gather.4.cloned.1.call-done) | copy-start | bytes 19169284
  96.4 131.9 %all-gather.8.cloned.1.call-start = ((), (), s32[]{:S(2)}) async-start(), calls=%async_computation.4 | async-start | bytes 4456448 | tf_op jit(solution)/shard_map/all_gather | solution.py:66
  143.2 14.3 %copy-start.4 = (bf16[8192,2,128]{2,0,1:T(8,128)(2,1)S(1)}, bf16[8192,2,128]{2,0,1:T(8,128)(2,1)}, u32[]{:S(2)}) copy-start(bf16[8192,2,128]{2,0,1:T(8,128)(2,1)} %all-gather.6.cloned.1.call-done) | copy-start | bytes 12582916
  157.5 70.9 %copy-start.3 = (bf16[1024,192]{0,1:T(8,128)(2,1)S(1)}, bf16[1024,192]{0,1:T(8,128)(2,1)}, u32[]{:S(2)}) copy-start(bf16[1024,192]{0,1:T(8,128)(2,1)} %copy-done.2) | copy-start | bytes 1179652
  157.5 70.8 %copy-start.5 = (bf16[2048,192]{0,1:T(8,128)(2,1)S(1)}, bf16[2048,192]{0,1:T(8,128)(2,1)}, u32[]{:S(2)}) copy-start(bf16[2048,192]{0,1:T(8,128)(2,1)} %copy_bitcast_fusion) | copy-start | bytes 2359300
Sparse Core Ops, SparseCore 0:
  12.1 70.7 all-gather.3
  96.6 31.9 all-gather.5
  171.8 56.4 all-gather.7
where the time goes:
time: 240 us; the launch traced here: 239 us
  waiting for transfers between devices  121 us (50%)
  matrix products  39.2 us (16%)
  blocking collectives  25.8 us (11%)
  other arithmetic  24.9 us (10%)
  between operations  13.9 us (6%)
  local copies, waits for them, and re-layouts  8.83 us (4%)
  starting transfers between devices  6.07 us (3%)
    all_gather x1, waiting for transfers between devices, body(): attended_full = lax.all_gather(attended, 'wid', axis=1, tiled=True)  56.4 us
    all_gather x1, waiting for transfers between devices, body(): key_values = lax.all_gather(qkv[:, 1:3], 'tok', axis=0, tiled=True)  31.9 us
    all_to_all x1, waiting for transfers between devices, body(): lax.all_to_all(w_copies, 'tok', split_axis=0, concat_axis=0, tiled=True)  28.9 us
    all_to_all x1, blocking collectives, body(): lax.all_to_all(w_out, 'wid', split_axis=1, concat_axis=0, tiled=True)  25.8 us
    dot_general x1, matrix products, body(): jnp.dot(queries, key_part.T, preferred_element_type=jnp.float32)  14.6 us
    reduce_sum x1, other arithmetic, body(): row_sum = jnp.sum(shifted, axis=1, keepdims=True)  14.3 us
    dot_general x1, matrix products, body(): jnp.dot(shifted.astype(jnp.bfloat16), value_part, preferred_element_type=...  14.2 us
    all_to_all x1, starting transfers between devices, body(): lax.all_to_all(w_copies, 'tok', split_axis=0, concat_axis=0, tiled=True)  5.81 us
  transfers between devices with their start and end apart: 4, of which 4 were waited for; matrix products, arithmetic and copies ran while one was open for 3% of the time, Pallas kernels for 0%

commit v1 on v0

--- a/solution.py
+++ b/solution.py
@@ -7,6 +7,27 @@
 D = 3072
 DH = 128
 TEMB = 256
+
+
+def gather_around(x, axis, dim):
+    devices, position, rows = (lax.axis_size(axis), lax.axis_index(axis), x.shape[dim])
+    right = [(i, (i + 1) % devices) for i in range(devices)]
+    left = [(i, (i - 1) % devices) for i in range(devices)]
+    whole = jnp.zeros((*x.shape[:dim], devices * rows, *x.shape[dim + 1 :]), x.dtype)
+    whole = lax.dynamic_update_slice_in_dim(whole, x, position * rows, axis=dim)
+    from_left = from_right = x
+    half = devices // 2
+    for step in range(1, half + 1):
+        from_left = lax.ppermute(from_left, axis, right)
+        whole = lax.dynamic_update_slice_in_dim(
+            whole, from_left, (position - step) % devices * rows, axis=dim
+        )
+        if step < devices - half:
+            from_right = lax.ppermute(from_right, axis, left)
+            whole = lax.dynamic_update_slice_in_dim(
+                whole, from_right, (position + step) % devices * rows, axis=dim
+            )
+    return whole
 
 
 def finish_rows(values, row_mean, row_var, shift_row, scale_row):
@@ -63,7 +84,7 @@
     row_sum = jnp.sum(shifted, axis=1, keepdims=True)
     numer = jnp.dot(shifted.astype(jnp.bfloat16), value_part, preferred_element_type=jnp.float32)
     attended = (numer / row_sum).astype(jnp.bfloat16)
-    attended_full = lax.all_gather(attended, "wid", axis=1, tiled=True)
+    attended_full = gather_around(attended, "wid", 1)
     projected = jnp.dot(attended_full, w_cols, preferred_element_type=jnp.float32)
     return (
         residual_in.astype(jnp.float32) + modulation[2].astype(jnp.float32)[None, :] * projected

time: 240 us -> 270 us (1.12)
  starting transfers between devices: 6.07 us -> 43.5 us
  waiting for transfers between devices: 121 us -> 98.9 us
  local copies, waits for them, and re-layouts: 8.83 us -> 22.8 us
    all_gather x1 -> x0, waiting for transfers between devices: 56.4 us -> none  [body(): attended_full = lax.all_gather(attended, 'wid', axis=1, tiled=True)]
    ppermute x0 -> x15, starting transfers between devices: none -> 37.6 us  [the longest x7 36.2 us: gather_around(): from_right = lax.ppermute(from_right, axis, left)]
    ppermute x0 -> x15, waiting for transfers between devices: none -> 33.6 us  [the longest x8 33.6 us: gather_around(): from_left = lax.ppermute(from_left, axis, right)]
    dynamic_update_slice x0 -> x15, local copies, waits for them, and re-layouts: none -> 11.3 us  [the longest x8 5.96 us: gather_around(): lax.dynamic_update_slice_in_dim(whole, from_left, (position - step) % dev...]
  transfers between devices with their start and end apart: 4 -> 18, of which waited for: 4 -> 11; matrix products, arithmetic and copies ran while one was open for 3% -> 6% of each run, Pallas kernels for 0% -> 0%
where the time goes in v1:
time: 270 us; the launch traced here: 269 us
  waiting for transfers between devices  98.9 us (37%)
  starting transfers between devices  43.5 us (16%)
  matrix products  39.2 us (15%)
  blocking collectives  25.8 us (10%)
  other arithmetic  24.6 us (9%)
  local copies, waits for them, and re-layouts  22.8 us (8%)
  between operations  14.5 us (5%)
    ppermute x7, starting transfers between devices, gather_around(): from_right = lax.ppermute(from_right, axis, left)  36.2 us
    ppermute x8, waiting for transfers between devices, gather_around(): from_left = lax.ppermute(from_left, axis, right)  33.6 us
    all_gather x1, waiting for transfers between devices, body(): key_values = lax.all_gather(qkv[:, 1:3], 'tok', axis=0, tiled=True)  32.1 us
    all_to_all x1, waiting for transfers between devices, body(): lax.all_to_all(w_copies, 'tok', split_axis=0, concat_axis=0, tiled=True)  28.9 us
    all_to_all x1, blocking collectives, body(): lax.all_to_all(w_out, 'wid', split_axis=1, concat_axis=0, tiled=True)  25.8 us
    dot_general x1, matrix products, body(): jnp.dot(queries, key_part.T, preferred_element_type=jnp.float32)  14.7 us
    dot_general x1, matrix products, body(): jnp.dot(shifted.astype(jnp.bfloat16), value_part, preferred_element_type=...  14.1 us
    reduce_sum x1, other arithmetic, body(): row_sum = jnp.sum(shifted, axis=1, keepdims=True)  14.1 us
  transfers between devices with their start and end apart: 18, of which 11 were waited for; matrix products, arithmetic and copies ran while one was open for 6% of the time, Pallas kernels for 0%

profile of v1, /device:TPU:0, one launch (start us, length us, event | category | flops | bytes accessed | tf_op | source)
XLA Modules:
  0.0 269.3 jit_solution(11899938288094163206)
XLA Ops:
  9.2 1.2 add_convert_fusion
  11.1 0.8 fusion.26
  12.0 1.5 copy.14
  13.5 25.8 %all_to_all.24 = bf16[128,16,192]{0,2,1:T(8,128)(2,1)S(1)} all-to-all(bf16[128,16,192]{0,2,1:T(8,128)(2,1)S(1)} %bitcast.43), channel_id=1, replica_groups=mesh['tok'=8,'wid'=16] {'wid'}, dimensions={1} | all-to-all | bytes 1572864 | tf_op jit(solution)/shard_map/all_to_all | solution.py:46
  39.3 2.0 broadcast_in_dim.5
  41.3 5.8 %all-to-all-start = ((bf16[8,384,3,128]{3,1,2,0:T(8,128)(2,1)}), bf16[8,384,3,128]{3,1,2,0:T(8,128)(2,1)S(1)}, u32[]{:S(2)}, u32[]{:S(2)}) async-start(bf16[8,384,3,128]{3,1,2,0:T(8,128)(2,1)} %broadcast_in_dim.5), calls=%async_computation | async-start | bytes 4718592 | tf_op jit(solution)/shard_map/all_to_all | solution.py:49
  47.2 1.0 copy_bitcast_fusion
  48.1 28.9 %all-to-all-done = bf16[8,384,3,128]{3,1,2,0:T(8,128)(2,1)S(1)} async-done(((bf16[8,384,3,128]{3,1,2,0:T(8,128)(2,1)}), bf16[8,384,3,128]{3,1,2,0:T(8,128)(2,1)S(1)}, u32[]{:S(2)}, u32[]{:S(2)}) %all-to-all-start) | async-done | bytes 2359328 | tf_op jit(solution)/shard_map/all_to_all | solution.py:49
  77.1 1.6 copy.12
  78.7 4.2 %all-gather.3.cloned.1.call-done = bf16[1040,3072]{0,1:T(8,128)(2,1)} async-done(((bf16[1040,192]{0,1:T(8,128)(2,1)}), bf16[1040,3072]{0,1:T(8,128)(2,1)}) %all-gather.3.cloned.1.call-update) | async-done | bytes 6389776 | tf_op jit(solution)/shard_map/all_gather | solution.py:62
  82.9 4.6 %convert_reduce_fusion = (f32[1024]{0:T(1024)S(1)}, f32[1024]{0:T(1024)S(1)}) fusion(bf16[1040,3072]{0,1:T(8,128)(2,1)} %all-gather.3.cloned.1.call-done), kind=kLoop, calls=%fused_computation.6 | loop fusion | flops 12580864 | bytes 6299648 | tf_op jit(solution)/shard_map/reduce_sum | solution.py:68
  87.5 2.3 add_reduce_fusion
  89.9 5.6 %fusion.14 = bf16[1024,3,128]{2,0,1:T(8,128)(2,1)S(1)} fusion(bf16[3072,3,128]{2,0,1:T(8,128)(2,1)} %bitcast.44, f32[3072]{0:T(1024)S(1)} %get-tuple-element.24, f32[3072]{0:T(1024)S(1)} %get-tuple-element.23, f32[1024]{0:T(1024)S(1)} %get-tuple-element.26, f32[1024]{0:T(1024)S(1)} %get-tuple-element.25, bf16[1040,3072]{0,1:T(8,128)(2,1)S(1)} %copy-done.2), kind=kOutput, calls=%fused_computation.21 | convolution fusion | flops 2435186688 | bytes 9469952 | tf_op jit(solution)/shard_map/td,dcf->tcf/dot_general | solution.py:73
  95.5 0.8 slice.52
  96.4 32.1 %all-gather.5.cloned.1.call-done = bf16[8192,2,128]{2,0,1:T(8,128)(2,1)} async-done(((bf16[1024,2,128]{2,0,1:T(8,128)(2,1)}), bf16[8192,2,128]{2,0,1:T(8,128)(2,1)}) %all-gather.5.cloned.1.call-update) | async-done | bytes 4194320 | tf_op jit(solution)/shard_map/all_gather | solution.py:78
  128.5 14.7 %multiply_reduce_fusion = (f32[1024]{0:T(1024)S(1)}, f32[1024,8192]{1,0:T(8,128)}) fusion(bf16[8192,2,128]{2,0,1:T(8,128)(2,1)} %all-gather.5.cloned.1.call-done, bf16[1024,3,128]{2,0,1:T(8,128)(2,1)S(1)} %fusion.14), kind=kOutput, calls=%fused_computation.1 | convolution fusion | flops 2164259840 | bytes 35917824 | tf_op jit(solution)/shard_map/dot_general | solution.py:82
  143.2 14.1 %fusion = f32[1024]{0:T(1024)S(1)} fusion(f32[1024,8192]{1,0:T(8,128)} %get-tuple-element.28, f32[1024]{0:T(1024)S(1)} %get-tuple-element.27), kind=kLoop, calls=%fused_computation.2 | loop fusion | flops 25164800 | bytes 33562624 | tf_op jit(solution)/shard_map/reduce_sum | solution.py:84
  157.2 2.7 broadcast_in_dim.4
  159.9 1.0 copy-done.5
  160.9 14.1 %constant_dynamic-update-slice_fusion.15 = (bf16[1024,2048]{1,0:T(8,128)(2,1)}, bf16[1024,128]{1,0:T(8,128)(2,1)S(1)}) fusion(bf16[1024,2048]{1,0:T(8,128)(2,1)} %broadcast_in_dim.4, s32[]{:T(128)S(6)} %select_n.111, f32[1024]{0:T(1024)S(1)} %fusion, bf16[8192,2,128]{2,0,1:T(8,128)(2,1)S(1)} %copy-done.5, f32[1024,8192]{1,0:T(8,128)} %get-tuple-element.28, ...), kind=kOutput, calls=%fused_computation.51 | convolution fusion | flops 2172911616 | bytes 36184068 | tf_op jit(solution)/shard_map/dot_general | solution.py:85
  175.0 1.4 collective-permute-start
  176.5 3.9 %collective-permute-start.1 = (bf16[1024,128]{1,0:T(8,128)(2,1)S(1)}, bf16[1024,128]{1,0:T(8,128)(2,1)S(1)}, u32[]{:S(2)}, u32[]{:S(2)}) collective-permute-start(bf16[1024,128]{1,0:T(8,128)(2,1)S(1)} %get-tuple-element.30), channel_id=1, source_target_pairs={{0,15},{1,0},{2,1},{3,2},{4,3},{5,4},{6,5},{7,6},{8,7},{9,8},{10,9... | collective-permute-start | bytes 786440 | tf_op jit(solution)/shard_map/ppermute | solution.py:26
  180.4 6.4 %collective-permute-done = bf16[1024,128]{1,0:T(8,128)(2,1)S(1)} collective-permute-done((bf16[1024,128]{1,0:T(8,128)(2,1)S(1)}, bf16[1024,128]{1,0:T(8,128)(2,1)S(1)}, u32[]{:S(2)}, u32[]{:S(2)}) %collective-permute-start) | collective-permute-done | bytes 262176 | tf_op jit(solution)/shard_map/ppermute | solution.py:21
  186.8 5.3 %collective-permute-start.3 = (bf16[1024,128]{1,0:T(8,128)(2,1)S(1)}, bf16[1024,128]{1,0:T(8,128)(2,1)S(1)}, u32[]{:S(2)}, u32[]{:S(2)}) collective-permute-start(bf16[1024,128]{1,0:T(8,128)(2,1)S(1)} %collective-permute-done.1), channel_id=1, source_target_pairs={{0,15},{1,0},{2,1},{3,2},{4,3},{5,4},{6,5},{7,6},{8,7},{9,8},{10,9... | collective-permute-start | bytes 786440 | tf_op jit(solution)/shard_map/ppermute | solution.py:26
  192.2 5.6 %collective-permute-done.2 = bf16[1024,128]{1,0:T(8,128)(2,1)S(1)} collective-permute-done((bf16[1024,128]{1,0:T(8,128)(2,1)S(1)}, bf16[1024,128]{1,0:T(8,128)(2,1)S(1)}, u32[]{:S(2)}, u32[]{:S(2)}) %collective-permute-start.2) | collective-permute-done | bytes 262176 | tf_op jit(solution)/shard_map/ppermute | solution.py:21
  197.7 5.3 %collective-permute-start.5 = (bf16[1024,128]{1,0:T(8,128)(2,1)S(1)}, bf16[1024,128]{1,0:T(8,128)(2,1)S(1)}, u32[]{:S(2)}, u32[]{:S(2)}) collective-permute-start(bf16[1024,128]{1,0:T(8,128)(2,1)S(1)} %collective-permute-done.3), channel_id=1, source_target_pairs={{0,15},{1,0},{2,1},{3,2},{4,3},{5,4},{6,5},{7,6},{8,7},{9,8},{10,9... | collective-permute-start | bytes 786440 | tf_op jit(solution)/shard_map/ppermute | solution.py:26
  203.1 4.7 %collective-permute-done.4 = bf16[1024,128]{1,0:T(8,128)(2,1)S(1)} collective-permute-done((bf16[1024,128]{1,0:T(8,128)(2,1)S(1)}, bf16[1024,128]{1,0:T(8,128)(2,1)S(1)}, u32[]{:S(2)}, u32[]{:S(2)}) %collective-permute-start.4) | collective-permute-done | bytes 262176 | tf_op jit(solution)/shard_map/ppermute | solution.py:21
  209.0 5.4 %collective-permute-start.7 = (bf16[1024,128]{1,0:T(8,128)(2,1)S(1)}, bf16[1024,128]{1,0:T(8,128)(2,1)S(1)}, u32[]{:S(2)}, u32[]{:S(2)}) collective-permute-start(bf16[1024,128]{1,0:T(8,128)(2,1)S(1)} %collective-permute-done.5), channel_id=1, source_target_pairs={{0,15},{1,0},{2,1},{3,2},{4,3},{5,4},{6,5},{7,6},{8,7},{9,8},{10,9... | collective-permute-start | bytes 786440 | tf_op jit(solution)/shard_map/ppermute | solution.py:26
  214.3 0.8 constant_dynamic-update-slice_fusion.13
  215.1 2.4 collective-permute-done.6
  219.0 5.4 %collective-permute-start.9 = (bf16[1024,128]{1,0:T(8,128)(2,1)S(1)}, bf16[1024,128]{1,0:T(8,128)(2,1)S(1)}, u32[]{:S(2)}, u32[]{:S(2)}) collective-permute-start(bf16[1024,128]{1,0:T(8,128)(2,1)S(1)} %collective-permute-done.7), channel_id=1, source_target_pairs={{0,15},{1,0},{2,1},{3,2},{4,3},{5,4},{6,5},{7,6},{8,7},{9,8},{10,9... | collective-permute-start | bytes 786440 | tf_op jit(solution)/shard_map/ppermute | solution.py:26
  224.3 0.8 constant_dynamic-update-slice_fusion.10
  225.1 2.1 collective-permute-done.8
  227.2 0.8 constant_dynamic-update-slice_fusion.9
  228.0 0.7 constant_dynamic-update-slice_fusion.8
  228.7 5.3 %collective-permute-start.11 = (bf16[1024,128]{1,0:T(8,128)(2,1)S(1)}, bf16[1024,128]{1,0:T(8,128)(2,1)S(1)}, u32[]{:S(2)}, u32[]{:S(2)}) collective-permute-start(bf16[1024,128]{1,0:T(8,128)(2,1)S(1)} %collective-permute-done.9), channel_id=1, source_target_pairs={{0,15},{1,0},{2,1},{3,2},{4,3},{5,4},{6,5},{7,6},{8,7},{9,8},{10,9... | collective-permute-start | bytes 786440 | tf_op jit(solution)/shard_map/ppermute | solution.py:26
  234.8 2.1 collective-permute-done.10
  236.9 0.7 constant_dynamic-update-slice_fusion.6
  237.6 0.7 constant_dynamic-update-slice_fusion.5
  238.4 5.5 %collective-permute-start.13 = (bf16[1024,128]{1,0:T(8,128)(2,1)S(1)}, bf16[1024,128]{1,0:T(8,128)(2,1)S(1)}, u32[]{:S(2)}, u32[]{:S(2)}) collective-permute-start(bf16[1024,128]{1,0:T(8,128)(2,1)S(1)} %collective-permute-done.11), channel_id=1, source_target_pairs={{0,15},{1,0},{2,1},{3,2},{4,3},{5,4},{6,5},{7,6},{8,7},{9,8},{10,9... | collective-permute-start | bytes 786440 | tf_op jit(solution)/shard_map/ppermute | solution.py:26
  243.9 0.8 constant_dynamic-update-slice_fusion.4
  244.6 2.9 %collective-permute-done.12 = bf16[1024,128]{1,0:T(8,128)(2,1)S(1)} collective-permute-done((bf16[1024,128]{1,0:T(8,128)(2,1)S(1)}, bf16[1024,128]{1,0:T(8,128)(2,1)S(1)}, u32[]{:S(2)}, u32[]{:S(2)}) %collective-permute-start.12) | collective-permute-done | bytes 262176 | tf_op jit(solution)/shard_map/ppermute | solution.py:21
  247.6 0.8 constant_dynamic-update-slice_fusion.3
  248.3 0.7 constant_dynamic-update-slice_fusion.2
  249.1 0.8 constant_dynamic-update-slice_fusion.1
  249.9 7.4 %collective-permute-done.14 = bf16[1024,128]{1,0:T(8,128)(2,1)S(1)} collective-permute-done((bf16[1024,128]{1,0:T(8,128)(2,1)S(1)}, bf16[1024,128]{1,0:T(8,128)(2,1)S(1)}, u32[]{:S(2)}, u32[]{:S(2)}) %collective-permute-start.14) | collective-permute-done | bytes 262176 | tf_op jit(solution)/shard_map/ppermute | solution.py:21
  257.3 0.7 constant_dynamic-update-slice_fusion
  258.0 4.5 %fusion.18 = bf16[1024,192]{0,1:T(8,128)(2,1)} fusion(bf16[1024,2048]{1,0:T(8,128)(2,1)} %constant_dynamic-update-slice_fusion, bf16[2048,192]{0,1:T(8,128)(2,1)S(1)} %copy-done.6, bf16[1024,192]{0,1:T(8,128)(2,1)S(1)} %copy-done.4, f32[192]{0:T(256)S(1)} %convert_reduce_fusion.2), kind=kOutput, calls=%fused_computation.24 | convolution fusion | flops 806092800 | bytes 5767936 | tf_op jit(solution)/shard_map/dot_general | solution.py:88
  (45 shorter events, 5.9 us)
Async XLA Ops:
  6.5 2.1 copy-start
  6.5 32.8 %copy-start.7 = (bf16[384,3,128]{2,0,1:T(8,128)(2,1)S(1)}, bf16[384,3,128]{2,0,1:T(8,128)(2,1)}, u32[]{:S(2)}) copy-start(bf16[384,3,128]{2,0,1:T(8,128)(2,1)} %param.14) | copy-start | bytes 884740
  6.5 76.4 %all-gather.3.cloned.1.call-start = ((), (), s32[]{:S(2)}) async-start(), calls=%async_computation.2 | async-start | bytes 7520256 | tf_op jit(solution)/shard_map/all_gather | solution.py:62
  10.4 0.7 copy-start.3
  41.3 35.8 %all-to-all-start = ((bf16[8,384,3,128]{3,1,2,0:T(8,128)(2,1)}), bf16[8,384,3,128]{3,1,2,0:T(8,128)(2,1)S(1)}, u32[]{:S(2)}, u32[]{:S(2)}) async-start(bf16[8,384,3,128]{3,1,2,0:T(8,128)(2,1)} %broadcast_in_dim.5), calls=%async_computation | async-start | bytes 4718592 | tf_op jit(solution)/shard_map/all_to_all | solution.py:49
  47.1 81.4 %all-gather.5.cloned.1.call-start = ((), (), s32[]{:S(2)}) async-start(), calls=%async_computation.3 | async-start | bytes 4718592 | tf_op jit(solution)/shard_map/all_gather | solution.py:78
  82.9 7.0 %copy-start.2 = (bf16[1040,3072]{0,1:T(8,128)(2,1)S(1)}, bf16[1040,3072]{0,1:T(8,128)(2,1)}, u32[]{:S(2)}) copy-start(bf16[1040,3072]{0,1:T(8,128)(2,1)} %all-gather.3.cloned.1.call-done) | copy-start | bytes 19169284
  157.2 3.7 %copy-start.5 = (bf16[8192,2,128]{2,0,1:T(8,128)(2,1)S(1)}, bf16[8192,2,128]{2,0,1:T(8,128)(2,1)}, u32[]{:S(2)}) copy-start(bf16[8192,2,128]{2,0,1:T(8,128)(2,1)} %all-gather.5.cloned.1.call-done) | copy-start | bytes 12582916
  175.0 83.0 %copy-start.4 = (bf16[1024,192]{0,1:T(8,128)(2,1)S(1)}, bf16[1024,192]{0,1:T(8,128)(2,1)}, u32[]{:S(2)}) copy-start(bf16[1024,192]{0,1:T(8,128)(2,1)} %copy-done.3) | copy-start | bytes 1179652
  175.0 83.0 %copy-start.6 = (bf16[2048,192]{0,1:T(8,128)(2,1)S(1)}, bf16[2048,192]{0,1:T(8,128)(2,1)}, u32[]{:S(2)}) copy-start(bf16[2048,192]{0,1:T(8,128)(2,1)} %copy_bitcast_fusion) | copy-start | bytes 2359300
  175.0 11.8 %collective-permute-start = (bf16[1024,128]{1,0:T(8,128)(2,1)S(1)}, bf16[1024,128]{1,0:T(8,128)(2,1)S(1)}, u32[]{:S(2)}, u32[]{:S(2)}) collective-permute-start(bf16[1024,128]{1,0:T(8,128)(2,1)S(1)} %get-tuple-element.30), channel_id=1, source_target_pairs={{0,1},{1,2},{2,3},{3,4},{4,5},{5,6},{6,7},{7,8},{8,9},{9,10},{10,1... | collective-permute-start | bytes 786440 | tf_op jit(solution)/shard_map/ppermute | solution.py:21
  176.5 10.3 %collective-permute-start.1 = (bf16[1024,128]{1,0:T(8,128)(2,1)S(1)}, bf16[1024,128]{1,0:T(8,128)(2,1)S(1)}, u32[]{:S(2)}, u32[]{:S(2)}) collective-permute-start(bf16[1024,128]{1,0:T(8,128)(2,1)S(1)} %get-tuple-element.30), channel_id=1, source_target_pairs={{0,15},{1,0},{2,1},{3,2},{4,3},{5,4},{6,5},{7,6},{8,7},{9,8},{10,9... | collective-permute-start | bytes 786440 | tf_op jit(solution)/shard_map/ppermute | solution.py:26
  186.8 10.9 %collective-permute-start.2 = (bf16[1024,128]{1,0:T(8,128)(2,1)S(1)}, bf16[1024,128]{1,0:T(8,128)(2,1)S(1)}, u32[]{:S(2)}, u32[]{:S(2)}) collective-permute-start(bf16[1024,128]{1,0:T(8,128)(2,1)S(1)} %collective-permute-done), channel_id=1, source_target_pairs={{0,1},{1,2},{2,3},{3,4},{4,5},{5,6},{6,7},{7,8},{8,9},{9,10},{10,1... | collective-permute-start | bytes 786440 | tf_op jit(solution)/shard_map/ppermute | solution.py:21
  186.8 10.9 %collective-permute-start.3 = (bf16[1024,128]{1,0:T(8,128)(2,1)S(1)}, bf16[1024,128]{1,0:T(8,128)(2,1)S(1)}, u32[]{:S(2)}, u32[]{:S(2)}) collective-permute-start(bf16[1024,128]{1,0:T(8,128)(2,1)S(1)} %collective-permute-done.1), channel_id=1, source_target_pairs={{0,15},{1,0},{2,1},{3,2},{4,3},{5,4},{6,5},{7,6},{8,7},{9,8},{10,9... | collective-permute-start | bytes 786440 | tf_op jit(solution)/shard_map/ppermute | solution.py:26
  197.7 10.1 %collective-permute-start.4 = (bf16[1024,128]{1,0:T(8,128)(2,1)S(1)}, bf16[1024,128]{1,0:T(8,128)(2,1)S(1)}, u32[]{:S(2)}, u32[]{:S(2)}) collective-permute-start(bf16[1024,128]{1,0:T(8,128)(2,1)S(1)} %collective-permute-done.2), channel_id=1, source_target_pairs={{0,1},{1,2},{2,3},{3,4},{4,5},{5,6},{6,7},{7,8},{8,9},{9,10},{10,1... | collective-permute-start | bytes 786440 | tf_op jit(solution)/shard_map/ppermute | solution.py:21
  197.7 11.2 %collective-permute-start.5 = (bf16[1024,128]{1,0:T(8,128)(2,1)S(1)}, bf16[1024,128]{1,0:T(8,128)(2,1)S(1)}, u32[]{:S(2)}, u32[]{:S(2)}) collective-permute-start(bf16[1024,128]{1,0:T(8,128)(2,1)S(1)} %collective-permute-done.3), channel_id=1, source_target_pairs={{0,15},{1,0},{2,1},{3,2},{4,3},{5,4},{6,5},{7,6},{8,7},{9,8},{10,9... | collective-permute-start | bytes 786440 | tf_op jit(solution)/shard_map/ppermute | solution.py:26
  207.8 9.7 %collective-permute-start.6 = (bf16[1024,128]{1,0:T(8,128)(2,1)S(1)}, bf16[1024,128]{1,0:T(8,128)(2,1)S(1)}, u32[]{:S(2)}, u32[]{:S(2)}) collective-permute-start(bf16[1024,128]{1,0:T(8,128)(2,1)S(1)} %collective-permute-done.4), channel_id=1, source_target_pairs={{0,1},{1,2},{2,3},{3,4},{4,5},{5,6},{6,7},{7,8},{8,9},{9,10},{10,1... | collective-permute-start | bytes 786440 | tf_op jit(solution)/shard_map/ppermute | solution.py:21
  209.0 10.0 %collective-permute-start.7 = (bf16[1024,128]{1,0:T(8,128)(2,1)S(1)}, bf16[1024,128]{1,0:T(8,128)(2,1)S(1)}, u32[]{:S(2)}, u32[]{:S(2)}) collective-permute-start(bf16[1024,128]{1,0:T(8,128)(2,1)S(1)} %collective-permute-done.5), channel_id=1, source_target_pairs={{0,15},{1,0},{2,1},{3,2},{4,3},{5,4},{6,5},{7,6},{8,7},{9,8},{10,9... | collective-permute-start | bytes 786440 | tf_op jit(solution)/shard_map/ppermute | solution.py:26
  217.5 9.7 %collective-permute-start.8 = (bf16[1024,128]{1,0:T(8,128)(2,1)S(1)}, bf16[1024,128]{1,0:T(8,128)(2,1)S(1)}, u32[]{:S(2)}, u32[]{:S(2)}) collective-permute-start(bf16[1024,128]{1,0:T(8,128)(2,1)S(1)} %collective-permute-done.6), channel_id=1, source_target_pairs={{0,1},{1,2},{2,3},{3,4},{4,5},{5,6},{6,7},{7,8},{8,9},{9,10},{10,1... | collective-permute-start | bytes 786440 | tf_op jit(solution)/shard_map/ppermute | solution.py:21
  219.0 9.7 %collective-permute-start.9 = (bf16[1024,128]{1,0:T(8,128)(2,1)S(1)}, bf16[1024,128]{1,0:T(8,128)(2,1)S(1)}, u32[]{:S(2)}, u32[]{:S(2)}) collective-permute-start(bf16[1024,128]{1,0:T(8,128)(2,1)S(1)} %collective-permute-done.7), channel_id=1, source_target_pairs={{0,15},{1,0},{2,1},{3,2},{4,3},{5,4},{6,5},{7,6},{8,7},{9,8},{10,9... | collective-permute-start | bytes 786440 | tf_op jit(solution)/shard_map/ppermute | solution.py:26
  227.2 9.7 %collective-permute-start.10 = (bf16[1024,128]{1,0:T(8,128)(2,1)S(1)}, bf16[1024,128]{1,0:T(8,128)(2,1)S(1)}, u32[]{:S(2)}, u32[]{:S(2)}) collective-permute-start(bf16[1024,128]{1,0:T(8,128)(2,1)S(1)} %collective-permute-done.8), channel_id=1, source_target_pairs={{0,1},{1,2},{2,3},{3,4},{4,5},{5,6},{6,7},{7,8},{8,9},{9,10},{10,1... | collective-permute-start | bytes 786440 | tf_op jit(solution)/shard_map/ppermute | solution.py:21
  228.7 9.7 %collective-permute-start.11 = (bf16[1024,128]{1,0:T(8,128)(2,1)S(1)}, bf16[1024,128]{1,0:T(8,128)(2,1)S(1)}, u32[]{:S(2)}, u32[]{:S(2)}) collective-permute-start(bf16[1024,128]{1,0:T(8,128)(2,1)S(1)} %collective-permute-done.9), channel_id=1, source_target_pairs={{0,15},{1,0},{2,1},{3,2},{4,3},{5,4},{6,5},{7,6},{8,7},{9,8},{10,9... | collective-permute-start | bytes 786440 | tf_op jit(solution)/shard_map/ppermute | solution.py:26
  236.9 10.7 %collective-permute-start.12 = (bf16[1024,128]{1,0:T(8,128)(2,1)S(1)}, bf16[1024,128]{1,0:T(8,128)(2,1)S(1)}, u32[]{:S(2)}, u32[]{:S(2)}) collective-permute-start(bf16[1024,128]{1,0:T(8,128)(2,1)S(1)} %collective-permute-done.10), channel_id=1, source_target_pairs={{0,1},{1,2},{2,3},{3,4},{4,5},{5,6},{6,7},{7,8},{8,9},{9,10},{10,1... | collective-permute-start | bytes 786440 | tf_op jit(solution)/shard_map/ppermute | solution.py:21
  238.4 10.7 %collective-permute-start.13 = (bf16[1024,128]{1,0:T(8,128)(2,1)S(1)}, bf16[1024,128]{1,0:T(8,128)(2,1)S(1)}, u32[]{:S(2)}, u32[]{:S(2)}) collective-permute-start(bf16[1024,128]{1,0:T(8,128)(2,1)S(1)} %collective-permute-done.11), channel_id=1, source_target_pairs={{0,15},{1,0},{2,1},{3,2},{4,3},{5,4},{6,5},{7,6},{8,7},{9,8},{10,9... | collective-permute-start | bytes 786440 | tf_op jit(solution)/shard_map/ppermute | solution.py:26
  247.6 9.7 %collective-permute-start.14 = (bf16[1024,128]{1,0:T(8,128)(2,1)S(1)}, bf16[1024,128]{1,0:T(8,128)(2,1)S(1)}, u32[]{:S(2)}, u32[]{:S(2)}) collective-permute-start(bf16[1024,128]{1,0:T(8,128)(2,1)S(1)} %collective-permute-done.12), channel_id=1, source_target_pairs={{0,1},{1,2},{2,3},{3,4},{4,5},{5,6},{6,7},{7,8},{8,9},{9,10},{10,1... | collective-permute-start | bytes 786440 | tf_op jit(solution)/shard_map/ppermute | solution.py:21
  247.6 14.9 %copy-start.1 = (bf16[256,3,192]{0,2,1:T(8,128)(2,1)S(1)}, bf16[256,3,192]{0,2,1:T(8,128)(2,1)}, u32[]{:S(2)}) copy-start(bf16[256,3,192]{0,2,1:T(8,128)(2,1)} %param.13) | copy-start | bytes 884740
Sparse Core Ops, SparseCore 0:
  12.1 70.7 all-gather.2
  96.5 31.9 all-gather.4
